TPU v7x, 32 devices: a whole 2x2x4 slice. The times are simulated.
32 devices in a mesh: outer: 4 (over y, x), inner: 8 (over z, core).
Axes of the slice: x: 2, y: 2, z: 4, core: 2. Of those that a mesh axis runs over, the one named last changes fastest.
Arguments:
- tokens: bfloat16 [4096, 2048], P(('outer', 'inner')), may hold values from -6 to 6
- cotangent: bfloat16 [4096, 2048], P(('outer', 'inner')), may hold values from -6 to 6
- routes: int32 [4096, 8], P(('outer', 'inner')), may hold values from 0 to 31, all different within a row; in each aligned block of 128 rows (0 to 127, 128 to 255, ...) at most 36 rows name the same one
- router_weight: bfloat16 [2048, 32], replicated, may hold values from -0.125 to 0.125
- gate_saved: bfloat16 [32, 1152, 768], P(('outer', 'inner')), may hold values from -6 to 6
- up_saved: bfloat16 [32, 1152, 768], P(('outer', 'inner')), may hold values from -6 to 6
- gate_weight: bfloat16 [32, 2048, 768], P(('outer', 'inner')), may hold values from -0.125 to 0.125
- up_weight: bfloat16 [32, 2048, 768], P(('outer', 'inner')), may hold values from -0.125 to 0.125
- down_weight: bfloat16 [32, 768, 2048], P(('outer', 'inner')), may hold values from -0.21875 to 0.21875
Outputs:
- grad_tokens: bfloat16 [4096, 2048], P(('outer', 'inner'))
- grad_gate: bfloat16 [32, 2048, 768], P(('outer', 'inner'))
- grad_up: bfloat16 [32, 2048, 768], P(('outer', 'inner'))
- grad_down: bfloat16 [32, 768, 2048], P(('outer', 'inner'))
- grad_router: float32 [2048, 32], replicated
Inputs may be any that keep to these rules, and one draw needn't show every extreme that they name: `routes`: each row names 8 different experts. Among the rows of one device no expert is named more than 36 times, and in every draw some expert is named exactly 36 times by the rows of some device.
All inputs are finite; a program needn't handle non-finite values.
Results may differ from a plain program's by a relative error of at most 0.01.
Values may be sent and summed in bfloat16 or wider, within the bound.
No kernel may reach another device: no remote copies, remote signals or barrier semaphores. Data moves between devices by JAX's collectives and lax.ppermute only.
A program may use at most 192 MiB of HBM per device.

v0:
```python
import math
import jax
import jax.numpy as jnp
from jax import lax
from jax.sharding import PartitionSpec as P

contract_rows = (((0,), (0,)), ((), ()))
contract_cols = (((1,), (1,)), ((), ()))


def route_tables(routes, experts, capacity):
    flat_routes = routes.reshape(-1)
    onehot = (flat_routes[:, None] == jnp.arange(experts, dtype=jnp.int32)[None, :]).astype(
        jnp.int32
    )
    earlier = jnp.cumsum(onehot, axis=0) - onehot
    position = jnp.sum(earlier * onehot, axis=1)
    target = flat_routes * capacity + position
    slot_table = (
        jnp.arange(experts * capacity, dtype=jnp.int32)[:, None] == target[None, :]
    ).astype(jnp.bfloat16)
    token_table = jnp.sum(
        slot_table.reshape(experts * capacity, routes.shape[0], routes.shape[1]), axis=2
    )
    return (slot_table, token_table)


def route_probs(tokens, routes, router_weight):
    router_logits = jnp.dot(tokens, router_weight, preferred_element_type=jnp.float32)
    picked = (
        routes[:, :, None] == jnp.arange(router_weight.shape[1], dtype=jnp.int32)[None, None, :]
    )
    chosen = jnp.sum(jnp.where(picked, router_logits[:, None, :], jnp.float32(0.0)), axis=2)
    exp_terms = jnp.exp(chosen)
    return (picked, exp_terms / jnp.sum(exp_terms, axis=1, keepdims=True))


def dispatch_block(tokens, cotangent, routes, router_weight, capacity):
    picked, probs = route_probs(tokens, routes, router_weight)
    slot_table, token_table = route_tables(routes, router_weight.shape[1], capacity)
    send_tokens = jnp.dot(token_table, tokens, preferred_element_type=jnp.float32).astype(
        jnp.bfloat16
    )
    send_cot = jnp.dot(token_table, cotangent, preferred_element_type=jnp.float32).astype(
        jnp.bfloat16
    )
    probs_low = probs.astype(jnp.bfloat16).reshape(-1)
    send_weight = jnp.dot(slot_table, probs_low, preferred_element_type=jnp.float32).astype(
        jnp.bfloat16
    )
    return (picked, probs, slot_table, token_table, send_tokens, send_cot, send_weight)


def slot_dot(cot_rows, out_rows):
    return jnp.sum(cot_rows.astype(jnp.float32) * out_rows.astype(jnp.float32), axis=1).astype(
        jnp.bfloat16
    )


def expert_backward(
    input_rows, cot_rows, weight_rows, gate_pre, up_pre, gate_matrix, up_matrix, down_matrix
):
    gate_value = gate_pre.astype(jnp.float32)
    up_value = up_pre.astype(jnp.float32)
    sigmoid_gate = jax.nn.sigmoid(gate_value)
    silu_gate = gate_value * sigmoid_gate
    hidden = (silu_gate * up_value).astype(jnp.bfloat16)
    expert_out = jnp.dot(hidden, down_matrix, preferred_element_type=jnp.float32).astype(
        jnp.bfloat16
    )
    scaled_cot = (weight_rows.astype(jnp.float32)[:, None] * cot_rows.astype(jnp.float32)).astype(
        jnp.bfloat16
    )
    grad_hidden = lax.dot_general(
        scaled_cot, down_matrix, contract_cols, preferred_element_type=jnp.float32
    )
    grad_gate_pre = (
        grad_hidden * up_value * sigmoid_gate * (1.0 + gate_value * (1.0 - sigmoid_gate))
    ).astype(jnp.bfloat16)
    grad_up_pre = (grad_hidden * silu_gate).astype(jnp.bfloat16)
    grad_rows = (
        lax.dot_general(
            grad_gate_pre, gate_matrix, contract_cols, preferred_element_type=jnp.float32
        )
        + lax.dot_general(grad_up_pre, up_matrix, contract_cols, preferred_element_type=jnp.float32)
    ).astype(jnp.bfloat16)
    grad_gate_w = lax.dot_general(
        input_rows, grad_gate_pre, contract_rows, preferred_element_type=jnp.float32
    ).astype(jnp.bfloat16)
    grad_up_w = lax.dot_general(
        input_rows, grad_up_pre, contract_rows, preferred_element_type=jnp.float32
    ).astype(jnp.bfloat16)
    grad_down_w = lax.dot_general(
        hidden, scaled_cot, contract_rows, preferred_element_type=jnp.float32
    ).astype(jnp.bfloat16)
    return (grad_rows, expert_out, grad_gate_w, grad_up_w, grad_down_w)


def finish_block(
    tokens, router_weight, picked, probs, slot_table, token_table, back_rows, route_dot
):
    grad_sum = lax.dot_general(
        token_table, back_rows, contract_rows, preferred_element_type=jnp.float32
    )
    route_grad = lax.dot_general(
        slot_table, route_dot, contract_rows, preferred_element_type=jnp.float32
    ).reshape(probs.shape)
    inner_term = jnp.sum(probs * route_grad, axis=1, keepdims=True)
    chosen_grad = probs * (route_grad - inner_term)
    logit_grad = jnp.sum(
        jnp.where(picked, chosen_grad[:, :, None], jnp.float32(0.0)), axis=1
    ).astype(jnp.bfloat16)
    grad_tokens = (
        grad_sum
        + lax.dot_general(
            logit_grad, router_weight, contract_cols, preferred_element_type=jnp.float32
        )
    ).astype(jnp.bfloat16)
    router_part = lax.dot_general(
        tokens, logit_grad, contract_rows, preferred_element_type=jnp.float32
    )
    return (grad_tokens, router_part)


def body(
    tokens,
    cotangent,
    routes,
    router_weight,
    gate_saved,
    up_saved,
    gate_weight,
    up_weight,
    down_weight,
):
    experts = router_weight.shape[1]
    width = tokens.shape[1]
    capacity = gate_saved.shape[1] // experts
    outer_size = lax.axis_size("outer")
    inner_size = lax.axis_size("inner")
    picked, probs, slot_table, token_table, send_tokens, send_cot, send_weight = dispatch_block(
        tokens, cotangent, routes, router_weight, capacity
    )
    grid_tokens = send_tokens.reshape(experts, capacity, width)
    grid_cot = send_cot.reshape(experts, capacity, width)
    grid_weight = send_weight.reshape(experts, capacity)
    got_tokens, got_cot, got_weight = (
        lax.all_to_all(grid_tokens, ("outer", "inner"), split_axis=0, concat_axis=0, tiled=True),
        lax.all_to_all(grid_cot, ("outer", "inner"), split_axis=0, concat_axis=0, tiled=True),
        lax.all_to_all(grid_weight, ("outer", "inner"), split_axis=0, concat_axis=0, tiled=True),
    )
    cot_rows = got_cot.reshape(-1, width)
    grad_rows, expert_out, grad_gate_w, grad_up_w, grad_down_w = expert_backward(
        got_tokens.reshape(-1, width),
        cot_rows,
        got_weight.reshape(-1),
        gate_saved[0],
        up_saved[0],
        gate_weight[0],
        up_weight[0],
        down_weight[0],
    )
    back_grad = grad_rows.reshape(experts, capacity, width)
    extra = expert_out.reshape(experts, capacity, width)
    back_rows, back_extra = (
        lax.all_to_all(back_grad, ("outer", "inner"), split_axis=0, concat_axis=0, tiled=True),
        lax.all_to_all(extra, ("outer", "inner"), split_axis=0, concat_axis=0, tiled=True),
    )
    route_dot = slot_dot(send_cot, back_extra.reshape(-1, width))
    grad_tokens, router_part = finish_block(
        tokens,
        router_weight,
        picked,
        probs,
        slot_table,
        token_table,
        back_rows.reshape(-1, width),
        route_dot,
    )
    total_tokens = tokens.shape[0] * outer_size * inner_size
    grad_router = lax.psum(router_part, ("outer", "inner")) * (1.0 / math.sqrt(total_tokens))
    return (grad_tokens, grad_gate_w[None], grad_up_w[None], grad_down_w[None], grad_router)


def solution(mesh):
    in_specs = (
        P(("outer", "inner"), None),
        P(("outer", "inner"), None),
        P(("outer", "inner"), None),
        P(),
        P(("outer", "inner"), None, None),
        P(("outer", "inner"), None, None),
        P(("outer", "inner"), None, None),
        P(("outer", "inner"), None, None),
        P(("outer", "inner"), None, None),
    )
    out_specs = (
        P(("outer", "inner"), None),
        P(("outer", "inner"), None, None),
        P(("outer", "inner"), None, None),
        P(("outer", "inner"), None, None),
        P(),
    )
    return jax.shard_map(body, mesh=mesh, in_specs=in_specs, out_specs=out_specs, check_vma=False)
```

profile of v0, /device:TPU:0, one launch (start us, length us, event | category | flops | bytes accessed | tf_op | source)
XLA Modules:
  0.0 628.6 jit_solution(13599808058669787535)
XLA Ops:
  7.2 1.9 copy-done
  9.1 8.1 %convolution_convert_fusion = bf16[1152,2048]{1,0:T(8,128)(2,1)} fusion(bf16[1,768,2048]{2,1,0:T(8,128)(2,1)S(1)} %copy-done, bf16[1,1152,768]{2,1,0:T(8,128)(2,1)} %param.14, bf16[1,1152,768]{2,1,0:T(8,128)(2,1)} %param.13), kind=kOutput, calls=%fused_computation.3 | convolution fusion | flops 3633315840 | bytes 11403264 | tf_op jit(solution)/shard_map/dot_general | solution.py:68
  17.1 7.2 %reshape.153 = bf16[32,36,2048]{2,1,0:T(8,128)(2,1)} reshape(bf16[1152,2048]{1,0:T(8,128)(2,1)} %convolution_convert_fusion) | data formatting | bytes 9437184 | tf_op jit(solution)/shard_map/reshape | solution.py:164
  24.3 7.4 %all-to-all-start.3 = ((bf16[32,36,2048]{2,1,0:T(8,128)(2,1)}), bf16[32,36,2048]{2,1,0:T(8,128)(2,1)}, u32[]{:S(2)}, u32[]{:S(2)}) async-start(bf16[32,36,2048]{2,1,0:T(8,128)(2,1)} %reshape.153), calls=%async_computation.3 | async-start | bytes 10485760 | tf_op jit(solution)/shard_map/all_to_all | solution.py:167
  31.7 0.1 copy.53
  31.8 0.1 eq.63
  31.9 0.1 eq.59
  32.0 9.0 %reduce-window.6 = s32[32,8,128]{2,1,0:T(8,128)S(1)} reduce-window(s32[32,8,128]{2,1,0:T(8,128)S(1)} %fusion.39, s32[]{:T(128)} %constant.5.clone.1), window={size=1x1x128 pad=0_0x0_0x127_0}, to_apply=%region_0.1 | reduce-window | flops 4161536 | bytes 262148 | tf_op jit(solution)/shard_map/reduce-window
  41.1 0.1 slice.8
  41.2 0.1 copy.55
  41.4 0.1 broadcast_add_fusion
  41.7 1.3 fusion.47
  43.1 6.0 fusion.30
  49.1 100.1 %all-to-all-done.3 = bf16[32,36,2048]{2,1,0:T(8,128)(2,1)} async-done(((bf16[32,36,2048]{2,1,0:T(8,128)(2,1)}), bf16[32,36,2048]{2,1,0:T(8,128)(2,1)}, u32[]{:S(2)}, u32[]{:S(2)}) %all-to-all-start.3) | async-done | bytes 4718624 | tf_op jit(solution)/shard_map/all_to_all | solution.py:167
  149.2 8.0 %reshape.160 = f32[1152,2048]{1,0:T(8,128)} reshape(bf16[32,36,2048]{2,1,0:T(8,128)(2,1)} %all-to-all-done.3) | data formatting | bytes 14155776 | tf_op jit(solution)/shard_map/convert_element_type | solution.py:55
  157.2 7.5 %multiply_reduce_fusion = (bf16[1152]{0:T(1024)(128)(2,1)S(1)}, bf16[1152,2048]{1,0:T(8,128)(2,1)}) fusion(f32[1152,2048]{1,0:T(8,128)} %reshape.160, bf16[1152,128]{1,0:T(8,128)(2,1)S(1)} %fusion.30, bf16[128,2048]{1,0:T(8,128)(2,1)} %param.10), kind=kOutput, calls=%fused_computation.1 | convolution fusion | flops 613415808 | bytes 14977280 | tf_op jit(solution)/shard_map/dot_general | solution.py:44
  164.7 0.8 fusion.3
  165.6 0.1 reshape.154
  165.7 0.1 copy.58
  165.9 0.1 reshape.161
  166.0 0.9 fusion.35
  166.9 0.7 all_to_all.24
  167.6 2.5 all-to-all-start
  170.2 7.2 %reshape.150 = bf16[32,36,2048]{2,1,0:T(8,128)(2,1)} reshape(bf16[1152,2048]{1,0:T(8,128)(2,1)} %get-tuple-element.8) | data formatting | bytes 9437184 | tf_op jit(solution)/shard_map/reshape | solution.py:145
  177.4 5.9 all-to-all-start.1
  183.3 4.5 convolution_convert_fusion.1
  187.9 7.2 %reshape.155 = bf16[32,36,2048]{2,1,0:T(8,128)(2,1)} reshape(bf16[1152,2048]{1,0:T(8,128)(2,1)} %convolution_convert_fusion.1) | data formatting | bytes 9437184 | tf_op jit(solution)/shard_map/reshape | solution.py:144
  195.1 105.8 %all-to-all-done.1 = bf16[32,36,2048]{2,1,0:T(8,128)(2,1)} async-done(((bf16[32,36,2048]{2,1,0:T(8,128)(2,1)}), bf16[32,36,2048]{2,1,0:T(8,128)(2,1)}, u32[]{:S(2)}, u32[]{:S(2)}) %all-to-all-start.1) | async-done | bytes 4718624 | tf_op jit(solution)/shard_map/all_to_all | solution.py:149
  300.8 3.8 all-to-all-start.4
  304.6 5.6 multiply_convert_fusion
  310.3 7.3 %convert_element_type.128 = bf16[1152,2048]{1,0:T(8,128)(2,1)} reshape(bf16[32,36,2048]{2,1,0:T(8,128)(2,1)} %multiply_convert_fusion) | data formatting | bytes 9437184 | tf_op jit(solution)/shard_map/convert_element_type | solution.py:71
  317.6 9.1 %fusion.9 = (bf16[1152,768]{1,0:T(8,128)(2,1)S(1)}, f32[1152,768]{1,0:T(8,128)}) fusion(bf16[1,1152,768]{2,1,0:T(8,128)(2,1)} %param.14, bf16[1,1152,768]{2,1,0:T(8,128)(2,1)} %param.13, bf16[1152,2048]{1,0:T(8,128)(2,1)} %convert_element_type.128, bf16[1,768,2048]{2,1,0:T(8,128)(2,1)S(1)} %copy-done), kind=kOutput, calls=%fused_computation.22 | convolution fusion | flops 3634495488 | bytes 16711680 | tf_op jit(solution)/shard_map/dot_general | solution.py:74
  326.6 3.9 fusion.21
  330.6 8.1 %add_convert_fusion = bf16[1152,2048]{1,0:T(8,128)(2,1)} fusion(f32[1152,2048]{1,0:T(8,128)S(1)} %fusion.21, bf16[1,2048,768]{2,1,0:T(8,128)(2,1)S(1)} %copy-done.8, f32[1152,768]{1,0:T(8,128)} %get-tuple-element.10, bf16[1,1152,768]{2,1,0:T(8,128)(2,1)S(1)} %copy-done.10), kind=kOutput, calls=%fused_computation.2 | convolution fusion | flops 3634790400 | bytes 22609920 | tf_op jit(solution)/shard_map/dot_general | solution.py:85
  338.7 7.2 %reshape.151 = bf16[32,36,2048]{2,1,0:T(8,128)(2,1)} reshape(bf16[1152,2048]{1,0:T(8,128)(2,1)} %add_convert_fusion) | data formatting | bytes 9437184 | tf_op jit(solution)/shard_map/reshape | solution.py:163
  345.9 76.1 %all-to-all-done.4 = bf16[32,36,2048]{2,1,0:T(8,128)(2,1)} async-done(((bf16[32,36,2048]{2,1,0:T(8,128)(2,1)}), bf16[32,36,2048]{2,1,0:T(8,128)(2,1)}, u32[]{:S(2)}, u32[]{:S(2)}) %all-to-all-start.4) | async-done | bytes 4718624 | tf_op jit(solution)/shard_map/all_to_all | solution.py:148
  421.9 3.6 all-to-all-start.2
  425.5 0.3 all-reduce.2.cloned.1.call-start
  425.8 0.9 convolution_bitcast_fusion
  426.8 7.3 %reshape.156 = bf16[1152,2048]{1,0:T(8,128)(2,1)} reshape(bf16[32,36,2048]{2,1,0:T(8,128)(2,1)} %all-to-all-done.4) | data formatting | bytes 9437184 | tf_op jit(solution)/shard_map/reshape | solution.py:154
  434.0 150.4 %all-reduce.2.cloned.1.call-done = f32[2048,32]{0,1:T(8,128)} async-done(((f32[2048,32]{0,1:T(8,128)}), f32[2048,32]{0,1:T(8,128)}) %all-reduce.2.cloned.1.call-update) | async-done | bytes 262160 | tf_op jit(solution)/shard_map/psum | solution.py:181
  584.4 1.7 broadcast_multiply_fusion
  586.1 9.1 %fusion.26 = bf16[1,2048,768]{2,1,0:T(8,128)(2,1)} fusion(bf16[1152,2048]{1,0:T(8,128)(2,1)} %reshape.156, bf16[1152,768]{1,0:T(8,128)(2,1)} %copy-done.13), kind=kOutput, calls=%fused_computation.42 | convolution fusion | flops 3625451520 | bytes 9633792 | tf_op jit(solution)/shard_map/dot_general | solution.py:87
  595.2 8.5 %fusion.28 = bf16[1,768,2048]{2,1,0:T(8,128)(2,1)} fusion(bf16[1152,2048]{1,0:T(8,128)(2,1)} %convert_element_type.128, bf16[1,1152,768]{2,1,0:T(8,128)(2,1)S(1)} %copy-done.9, bf16[1,1152,768]{2,1,0:T(8,128)(2,1)S(1)} %copy-done.11), kind=kOutput, calls=%fused_computation.44 | convolution fusion | flops 3632529408 | bytes 11403264 | tf_op jit(solution)/shard_map/dot_general | solution.py:93
  603.7 6.3 %fusion.27 = bf16[1,2048,768]{2,1,0:T(8,128)(2,1)} fusion(bf16[1152,2048]{1,0:T(8,128)(2,1)S(1)} %copy-done.3, f32[1152,768]{1,0:T(8,128)S(1)} %copy-done.12, bf16[1,1152,768]{2,1,0:T(8,128)(2,1)S(1)} %copy-done.11), kind=kOutput, calls=%fused_computation.43 | convolution fusion | flops 3631644672 | bytes 13172736 | tf_op jit(solution)/shard_map/dot_general | solution.py:90
  609.9 7.4 %reshape.152 = bf16[1152,2048]{1,0:T(8,128)(2,1)} reshape(bf16[32,36,2048]{2,1,0:T(8,128)(2,1)} %all-to-all-done.2) | data formatting | bytes 9437184 | tf_op jit(solution)/shard_map/reshape | solution.py:177
  617.3 3.2 fusion.48
  620.6 1.1 fusion.29
  (47 shorter events, 0.6 us)
Async XLA Ops:
  7.2 1.9 copy-start
  24.3 7.4 %copy-start.6 = (s32[128,8]{0,1:T(8,128)S(1)}, s32[128,8]{0,1:T(8,128)}, u32[]{:S(2)}) copy-start(s32[128,8]{0,1:T(8,128)} %param.11) | copy-start | bytes 12292
  24.3 17.4 %copy-start.4 = (bf16[2048,32]{0,1:T(8,128)(2,1)S(1)}, bf16[2048,32]{0,1:T(8,128)(2,1)}, u32[]{:S(2)}) copy-start(bf16[2048,32]{0,1:T(8,128)(2,1)} %param.12) | copy-start | bytes 393220
  24.3 124.9 %all-to-all-start.3 = ((bf16[32,36,2048]{2,1,0:T(8,128)(2,1)}), bf16[32,36,2048]{2,1,0:T(8,128)(2,1)}, u32[]{:S(2)}, u32[]{:S(2)}) async-start(bf16[32,36,2048]{2,1,0:T(8,128)(2,1)} %reshape.153), calls=%async_computation.3 | async-start | bytes 10485760 | tf_op jit(solution)/shard_map/all_to_all | solution.py:167
  167.6 9.8 %all-to-all-start = ((bf16[32,1,36]{2,1,0:T(2,128)(2,1)}), bf16[32,1,36]{2,1,0:T(2,128)(2,1)S(1)}, u32[]{:S(2)}, u32[]{:S(2)}) async-start(bf16[32,1,36]{2,1,0:T(2,128)(2,1)} %all_to_all.24), calls=%async_computation | async-start | bytes 32768 | tf_op jit(solution)/shard_map/all_to_all | solution.py:150
  177.4 123.5 %all-to-all-start.1 = ((bf16[32,36,2048]{2,1,0:T(8,128)(2,1)}), bf16[32,36,2048]{2,1,0:T(8,128)(2,1)}, u32[]{:S(2)}, u32[]{:S(2)}) async-start(bf16[32,36,2048]{2,1,0:T(8,128)(2,1)} %reshape.150), calls=%async_computation.1 | async-start | bytes 10485760 | tf_op jit(solution)/shard_map/all_to_all | solution.py:149
  300.8 121.1 %all-to-all-start.4 = ((bf16[32,36,2048]{2,1,0:T(8,128)(2,1)}), bf16[32,36,2048]{2,1,0:T(8,128)(2,1)}, u32[]{:S(2)}, u32[]{:S(2)}) async-start(bf16[32,36,2048]{2,1,0:T(8,128)(2,1)} %reshape.155), calls=%async_computation.4 | async-start | bytes 10485760 | tf_op jit(solution)/shard_map/all_to_all | solution.py:148
  317.6 9.1 %copy-start.7 = (bf16[1,2048,768]{2,1,0:T(8,128)(2,1)S(1)}, bf16[1,2048,768]{2,1,0:T(8,128)(2,1)}, u32[]{:S(2)}) copy-start(bf16[1,2048,768]{2,1,0:T(8,128)(2,1)} %param.15) | copy-start | bytes 9437188
  326.6 3.9 copy-start.13
  326.6 3.9 copy-start.8
  326.6 3.9 copy-start.10
  345.9 80.0 %copy-start.2 = (bf16[128,2048]{1,0:T(8,128)(2,1)S(1)}, bf16[128,2048]{1,0:T(8,128)(2,1)}, u32[]{:S(2)}) copy-start(bf16[128,2048]{1,0:T(8,128)(2,1)} %param.9) | copy-start | bytes 1572868
  421.9 188.0 %all-to-all-start.2 = ((bf16[32,36,2048]{2,1,0:T(8,128)(2,1)}), bf16[32,36,2048]{2,1,0:T(8,128)(2,1)}, u32[]{:S(2)}, u32[]{:S(2)}) async-start(bf16[32,36,2048]{2,1,0:T(8,128)(2,1)} %reshape.151), calls=%async_computation.2 | async-start | bytes 10485760 | tf_op jit(solution)/shard_map/all_to_all | solution.py:166
  425.5 158.9 %all-reduce.2.cloned.1.call-start = ((), (), s32[]{:S(2)}) async-start(), calls=%async_computation.5 | async-start | bytes 524288 | tf_op jit(solution)/shard_map/psum | solution.py:181
  586.1 9.1 %copy-start.9 = (bf16[1,1152,768]{2,1,0:T(8,128)(2,1)S(1)}, bf16[1,1152,768]{2,1,0:T(8,128)(2,1)}, u32[]{:S(2)}) copy-start(bf16[1,1152,768]{2,1,0:T(8,128)(2,1)} %param.14) | copy-start | bytes 5308420
  586.1 9.1 %copy-start.11 = (bf16[1,1152,768]{2,1,0:T(8,128)(2,1)S(1)}, bf16[1,1152,768]{2,1,0:T(8,128)(2,1)}, u32[]{:S(2)}) copy-start(bf16[1,1152,768]{2,1,0:T(8,128)(2,1)} %param.13) | copy-start | bytes 5308420
  595.2 8.5 %copy-start.3 = (bf16[1152,2048]{1,0:T(8,128)(2,1)S(1)}, bf16[1152,2048]{1,0:T(8,128)(2,1)}, u32[]{:S(2)}) copy-start(bf16[1152,2048]{1,0:T(8,128)(2,1)} %reshape.156) | copy-start | bytes 14155780
  595.2 8.5 %copy-start.12 = (f32[1152,768]{1,0:T(8,128)S(1)}, f32[1152,768]{1,0:T(8,128)}, u32[]{:S(2)}) copy-start(f32[1152,768]{1,0:T(8,128)} %get-tuple-element.10) | copy-start | bytes 10616836
  609.9 11.8 %copy-start.1 = (bf16[1,768,2048]{2,1,0:T(8,128)(2,1)S(1)}, bf16[1,768,2048]{2,1,0:T(8,128)(2,1)}, u32[]{:S(2)}) copy-start(bf16[1,768,2048]{2,1,0:T(8,128)(2,1)} %param.17) | copy-start | bytes 9437188
  617.3 3.3 copy-start.5
Sparse Core Ops, SparseCore 0:
  432.4 151.9 all-reduce.1
where the time goes:
time: 630 us; the launch traced here: 629 us
  waiting for transfers between devices  432 us (69%)
  matrix products  73.2 us (12%)
  local copies, waits for them, and re-layouts  62.5 us (10%)
  starting transfers between devices  23.5 us (4%)
  other arithmetic  22.7 us (4%)
  between operations  14.3 us (2%)
    psum x1, waiting for transfers between devices, body(): lax.psum(router_part, ('outer', 'inner')) * (1.0 / math.sqrt(total_tokens))  150 us
    all_to_all x1, waiting for transfers between devices, body(): lax.all_to_all(grid_cot, ('outer', 'inner'), split_axis=0, concat_axis=0,...  106 us
    all_to_all x1, waiting for transfers between devices, body(): lax.all_to_all(extra, ('outer', 'inner'), split_axis=0, concat_axis=0, ti...  100 us
    all_to_all x1, waiting for transfers between devices, body(): lax.all_to_all(grid_tokens, ('outer', 'inner'), split_axis=0, concat_axis...  76.1 us
  transfers between devices with their start and end apart: 6, of which 4 were waited for; matrix products, arithmetic and copies ran while one was open for 18% of the time, Pallas kernels for 0%

commit v1 on v0

--- a/solution.py
+++ b/solution.py
@@ -178,7 +178,9 @@
         route_dot,
     )
     total_tokens = tokens.shape[0] * outer_size * inner_size
-    grad_router = lax.psum(router_part, ("outer", "inner")) * (1.0 / math.sqrt(total_tokens))
+    grad_router = lax.psum(lax.psum(router_part, "inner"), "outer") * (
+        1.0 / math.sqrt(total_tokens)
+    )
     return (grad_tokens, grad_gate_w[None], grad_up_w[None], grad_down_w[None], grad_router)
 
 

time: 630 us -> 597 us (0.948)
  waiting for transfers between devices: 432 us -> 399 us
    psum x1 -> x2, waiting for transfers between devices: 150 us -> 117 us  [the longest x1 77 us: body(): lax.psum(router_part, 'inner')]
  transfers between devices with their start and end apart: 6 -> 7, of which waited for: 4 -> 5; matrix products, arithmetic and copies ran while one was open for 18% -> 19% of each run, Pallas kernels for 0% -> 0%
where the time goes in v1:
time: 597 us; the launch traced here: 595 us
  waiting for transfers between devices  399 us (67%)
  matrix products  73.2 us (12%)
  local copies, waits for them, and re-layouts  62.5 us (10%)
  starting transfers between devices  23.5 us (4%)
  other arithmetic  22.7 us (4%)
  between operations  14.3 us (2%)
    all_to_all x1, waiting for transfers between devices, body(): lax.all_to_all(grid_cot, ('outer', 'inner'), split_axis=0, concat_axis=0,...  106 us
    all_to_all x1, waiting for transfers between devices, body(): lax.all_to_all(extra, ('outer', 'inner'), split_axis=0, concat_axis=0, ti...  100 us
    psum x1, waiting for transfers between devices, body(): lax.psum(router_part, 'inner')  77 us
    all_to_all x1, waiting for transfers between devices, body(): lax.all_to_all(grid_tokens, ('outer', 'inner'), split_axis=0, concat_axis...  76.1 us
    psum x1, waiting for transfers between devices, body(): lax.psum(lax.psum(router_part, 'inner'), 'outer')  40.2 us
  transfers between devices with their start and end apart: 7, of which 5 were waited for; matrix products, arithmetic and copies ran while one was open for 19% of the time, Pallas kernels for 0%

profile of v1, /device:TPU:0, one launch (start us, length us, event | category | flops | bytes accessed | tf_op | source)
XLA Modules:
  0.0 595.4 jit_solution(18427234429025240157)
XLA Ops:
  7.2 1.9 copy-done
  9.1 8.1 %convolution_convert_fusion = bf16[1152,2048]{1,0:T(8,128)(2,1)} fusion(bf16[1,768,2048]{2,1,0:T(8,128)(2,1)S(1)} %copy-done, bf16[1,1152,768]{2,1,0:T(8,128)(2,1)} %param.14, bf16[1,1152,768]{2,1,0:T(8,128)(2,1)} %param.13), kind=kOutput, calls=%fused_computation.3 | convolution fusion | flops 3633315840 | bytes 11403264 | tf_op jit(solution)/shard_map/dot_general | solution.py:68
  17.1 7.2 %reshape.153 = bf16[32,36,2048]{2,1,0:T(8,128)(2,1)} reshape(bf16[1152,2048]{1,0:T(8,128)(2,1)} %convolution_convert_fusion) | data formatting | bytes 9437184 | tf_op jit(solution)/shard_map/reshape | solution.py:164
  24.3 7.4 %all-to-all-start.3 = ((bf16[32,36,2048]{2,1,0:T(8,128)(2,1)}), bf16[32,36,2048]{2,1,0:T(8,128)(2,1)}, u32[]{:S(2)}, u32[]{:S(2)}) async-start(bf16[32,36,2048]{2,1,0:T(8,128)(2,1)} %reshape.153), calls=%async_computation.3 | async-start | bytes 10485760 | tf_op jit(solution)/shard_map/all_to_all | solution.py:167
  31.7 0.1 copy.53
  31.8 0.1 eq.63
  31.9 0.1 eq.59
  32.0 9.0 %reduce-window.6 = s32[32,8,128]{2,1,0:T(8,128)S(1)} reduce-window(s32[32,8,128]{2,1,0:T(8,128)S(1)} %fusion.39, s32[]{:T(128)} %constant.5.clone.1), window={size=1x1x128 pad=0_0x0_0x127_0}, to_apply=%region_0.1 | reduce-window | flops 4161536 | bytes 262148 | tf_op jit(solution)/shard_map/reduce-window
  41.1 0.1 slice.8
  41.2 0.1 copy.55
  41.4 0.1 broadcast_add_fusion
  41.7 1.3 fusion.47
  43.1 6.0 %fusion.30 = bf16[1152,128]{1,0:T(8,128)(2,1)S(1)} fusion(s32[128,8]{0,1:T(8,128)S(1)} %multiply_add_fusion.1), kind=kLoop, calls=%fused_computation.47 | loop fusion | flops 3391488 | bytes 299008 | tf_op jit(solution)/shard_map/reduce_sum | solution.py:22
  49.1 100.1 %all-to-all-done.3 = bf16[32,36,2048]{2,1,0:T(8,128)(2,1)} async-done(((bf16[32,36,2048]{2,1,0:T(8,128)(2,1)}), bf16[32,36,2048]{2,1,0:T(8,128)(2,1)}, u32[]{:S(2)}, u32[]{:S(2)}) %all-to-all-start.3) | async-done | bytes 4718624 | tf_op jit(solution)/shard_map/all_to_all | solution.py:167
  149.2 8.0 %reshape.160 = f32[1152,2048]{1,0:T(8,128)} reshape(bf16[32,36,2048]{2,1,0:T(8,128)(2,1)} %all-to-all-done.3) | data formatting | bytes 14155776 | tf_op jit(solution)/shard_map/convert_element_type | solution.py:55
  157.2 7.5 %multiply_reduce_fusion = (bf16[1152]{0:T(1024)(128)(2,1)S(1)}, bf16[1152,2048]{1,0:T(8,128)(2,1)}) fusion(f32[1152,2048]{1,0:T(8,128)} %reshape.160, bf16[1152,128]{1,0:T(8,128)(2,1)S(1)} %fusion.30, bf16[128,2048]{1,0:T(8,128)(2,1)} %param.10), kind=kOutput, calls=%fused_computation.1 | convolution fusion | flops 613415808 | bytes 14977280 | tf_op jit(solution)/shard_map/dot_general | solution.py:44
  164.7 0.8 fusion.3
  165.7 0.1 copy.58
  165.9 0.1 reshape.161
  166.0 0.9 fusion.35
  166.9 0.7 all_to_all.24
  167.6 2.5 all-to-all-start
  170.2 7.2 %reshape.150 = bf16[32,36,2048]{2,1,0:T(8,128)(2,1)} reshape(bf16[1152,2048]{1,0:T(8,128)(2,1)} %get-tuple-element.8) | data formatting | bytes 9437184 | tf_op jit(solution)/shard_map/reshape | solution.py:145
  177.4 5.9 all-to-all-start.1
  183.3 4.5 convolution_convert_fusion.1
  187.9 7.2 %reshape.155 = bf16[32,36,2048]{2,1,0:T(8,128)(2,1)} reshape(bf16[1152,2048]{1,0:T(8,128)(2,1)} %convolution_convert_fusion.1) | data formatting | bytes 9437184 | tf_op jit(solution)/shard_map/reshape | solution.py:144
  195.1 105.8 %all-to-all-done.1 = bf16[32,36,2048]{2,1,0:T(8,128)(2,1)} async-done(((bf16[32,36,2048]{2,1,0:T(8,128)(2,1)}), bf16[32,36,2048]{2,1,0:T(8,128)(2,1)}, u32[]{:S(2)}, u32[]{:S(2)}) %all-to-all-start.1) | async-done | bytes 4718624 | tf_op jit(solution)/shard_map/all_to_all | solution.py:149
  300.8 3.8 all-to-all-start.4
  304.6 5.6 multiply_convert_fusion
  310.3 7.3 %convert_element_type.128 = bf16[1152,2048]{1,0:T(8,128)(2,1)} reshape(bf16[32,36,2048]{2,1,0:T(8,128)(2,1)} %multiply_convert_fusion) | data formatting | bytes 9437184 | tf_op jit(solution)/shard_map/convert_element_type | solution.py:71
  317.6 9.0 %fusion.9 = (bf16[1152,768]{1,0:T(8,128)(2,1)S(1)}, f32[1152,768]{1,0:T(8,128)}) fusion(bf16[1,1152,768]{2,1,0:T(8,128)(2,1)} %param.14, bf16[1,1152,768]{2,1,0:T(8,128)(2,1)} %param.13, bf16[1152,2048]{1,0:T(8,128)(2,1)} %convert_element_type.128, bf16[1,768,2048]{2,1,0:T(8,128)(2,1)S(1)} %copy-done), kind=kOutput, calls=%fused_computation.22 | convolution fusion | flops 3634495488 | bytes 16711680 | tf_op jit(solution)/shard_map/dot_general | solution.py:74
  326.6 3.9 fusion.21
  330.6 8.1 %add_convert_fusion = bf16[1152,2048]{1,0:T(8,128)(2,1)} fusion(f32[1152,2048]{1,0:T(8,128)S(1)} %fusion.21, bf16[1,2048,768]{2,1,0:T(8,128)(2,1)S(1)} %copy-done.8, f32[1152,768]{1,0:T(8,128)} %get-tuple-element.10, bf16[1,1152,768]{2,1,0:T(8,128)(2,1)S(1)} %copy-done.10), kind=kOutput, calls=%fused_computation.2 | convolution fusion | flops 3634790400 | bytes 22609920 | tf_op jit(solution)/shard_map/dot_general | solution.py:85
  338.6 7.2 %reshape.151 = bf16[32,36,2048]{2,1,0:T(8,128)(2,1)} reshape(bf16[1152,2048]{1,0:T(8,128)(2,1)} %add_convert_fusion) | data formatting | bytes 9437184 | tf_op jit(solution)/shard_map/reshape | solution.py:163
  345.8 76.1 %all-to-all-done.4 = bf16[32,36,2048]{2,1,0:T(8,128)(2,1)} async-done(((bf16[32,36,2048]{2,1,0:T(8,128)(2,1)}), bf16[32,36,2048]{2,1,0:T(8,128)(2,1)}, u32[]{:S(2)}, u32[]{:S(2)}) %all-to-all-start.4) | async-done | bytes 4718624 | tf_op jit(solution)/shard_map/all_to_all | solution.py:148
  421.9 3.6 all-to-all-start.2
  425.6 0.9 convolution_bitcast_fusion
  426.6 0.3 all-reduce.5.cloned.1.call-start
  426.8 77.0 %all-reduce.3.cloned.1.call-done = f32[2048,32]{0,1:T(8,128)} async-done(((f32[2048,32]{0,1:T(8,128)}), f32[2048,32]{0,1:T(8,128)}) %all-reduce.3.cloned.1.call-update) | async-done | bytes 262160 | tf_op jit(solution)/shard_map/psum | solution.py:181
  503.9 7.2 %reshape.156 = bf16[1152,2048]{1,0:T(8,128)(2,1)} reshape(bf16[32,36,2048]{2,1,0:T(8,128)(2,1)} %all-to-all-done.4) | data formatting | bytes 9437184 | tf_op jit(solution)/shard_map/reshape | solution.py:154
  511.1 40.2 %all-reduce.5.cloned.1.call-done = f32[2048,32]{0,1:T(8,128)} async-done(((f32[2048,32]{0,1:T(8,128)}), f32[2048,32]{0,1:T(8,128)}) %all-reduce.5.cloned.1.call-update) | async-done | bytes 262160 | tf_op jit(solution)/shard_map/psum | solution.py:181
  551.3 1.7 broadcast_multiply_fusion
  553.0 9.1 %fusion.26 = bf16[1,2048,768]{2,1,0:T(8,128)(2,1)} fusion(bf16[1152,2048]{1,0:T(8,128)(2,1)} %reshape.156, bf16[1152,768]{1,0:T(8,128)(2,1)} %copy-done.13), kind=kOutput, calls=%fused_computation.42 | convolution fusion | flops 3625451520 | bytes 9633792 | tf_op jit(solution)/shard_map/dot_general | solution.py:87
  562.0 8.5 %fusion.28 = bf16[1,768,2048]{2,1,0:T(8,128)(2,1)} fusion(bf16[1152,2048]{1,0:T(8,128)(2,1)} %convert_element_type.128, bf16[1,1152,768]{2,1,0:T(8,128)(2,1)S(1)} %copy-done.9, bf16[1,1152,768]{2,1,0:T(8,128)(2,1)S(1)} %copy-done.11), kind=kOutput, calls=%fused_computation.44 | convolution fusion | flops 3632529408 | bytes 11403264 | tf_op jit(solution)/shard_map/dot_general | solution.py:93
  570.5 6.3 %fusion.27 = bf16[1,2048,768]{2,1,0:T(8,128)(2,1)} fusion(bf16[1152,2048]{1,0:T(8,128)(2,1)S(1)} %copy-done.3, f32[1152,768]{1,0:T(8,128)S(1)} %copy-done.12, bf16[1,1152,768]{2,1,0:T(8,128)(2,1)S(1)} %copy-done.11), kind=kOutput, calls=%fused_computation.43 | convolution fusion | flops 3631644672 | bytes 13172736 | tf_op jit(solution)/shard_map/dot_general | solution.py:90
  576.8 7.4 %reshape.152 = bf16[1152,2048]{1,0:T(8,128)(2,1)} reshape(bf16[32,36,2048]{2,1,0:T(8,128)(2,1)} %all-to-all-done.2) | data formatting | bytes 9437184 | tf_op jit(solution)/shard_map/reshape | solution.py:177
  584.2 3.2 fusion.48
  587.5 1.1 fusion.29
  (50 shorter events, 0.7 us)
Async XLA Ops:
  7.2 1.9 copy-start
  24.3 7.4 %copy-start.6 = (s32[128,8]{0,1:T(8,128)S(1)}, s32[128,8]{0,1:T(8,128)}, u32[]{:S(2)}) copy-start(s32[128,8]{0,1:T(8,128)} %param.11) | copy-start | bytes 12292
  24.3 17.4 %copy-start.4 = (bf16[2048,32]{0,1:T(8,128)(2,1)S(1)}, bf16[2048,32]{0,1:T(8,128)(2,1)}, u32[]{:S(2)}) copy-start(bf16[2048,32]{0,1:T(8,128)(2,1)} %param.12) | copy-start | bytes 393220
  24.3 124.9 %all-to-all-start.3 = ((bf16[32,36,2048]{2,1,0:T(8,128)(2,1)}), bf16[32,36,2048]{2,1,0:T(8,128)(2,1)}, u32[]{:S(2)}, u32[]{:S(2)}) async-start(bf16[32,36,2048]{2,1,0:T(8,128)(2,1)} %reshape.153), calls=%async_computation.3 | async-start | bytes 10485760 | tf_op jit(solution)/shard_map/all_to_all | solution.py:167
  167.6 9.8 %all-to-all-start = ((bf16[32,1,36]{2,1,0:T(2,128)(2,1)}), bf16[32,1,36]{2,1,0:T(2,128)(2,1)S(1)}, u32[]{:S(2)}, u32[]{:S(2)}) async-start(bf16[32,1,36]{2,1,0:T(2,128)(2,1)} %all_to_all.24), calls=%async_computation | async-start | bytes 32768 | tf_op jit(solution)/shard_map/all_to_all | solution.py:150
  177.4 123.5 %all-to-all-start.1 = ((bf16[32,36,2048]{2,1,0:T(8,128)(2,1)}), bf16[32,36,2048]{2,1,0:T(8,128)(2,1)}, u32[]{:S(2)}, u32[]{:S(2)}) async-start(bf16[32,36,2048]{2,1,0:T(8,128)(2,1)} %reshape.150), calls=%async_computation.1 | async-start | bytes 10485760 | tf_op jit(solution)/shard_map/all_to_all | solution.py:149
  300.8 121.1 %all-to-all-start.4 = ((bf16[32,36,2048]{2,1,0:T(8,128)(2,1)}), bf16[32,36,2048]{2,1,0:T(8,128)(2,1)}, u32[]{:S(2)}, u32[]{:S(2)}) async-start(bf16[32,36,2048]{2,1,0:T(8,128)(2,1)} %reshape.155), calls=%async_computation.4 | async-start | bytes 10485760 | tf_op jit(solution)/shard_map/all_to_all | solution.py:148
  317.6 9.0 %copy-start.7 = (bf16[1,2048,768]{2,1,0:T(8,128)(2,1)S(1)}, bf16[1,2048,768]{2,1,0:T(8,128)(2,1)}, u32[]{:S(2)}) copy-start(bf16[1,2048,768]{2,1,0:T(8,128)(2,1)} %param.15) | copy-start | bytes 9437188
  326.6 3.9 copy-start.13
  326.6 3.9 copy-start.8
  326.6 3.9 copy-start.10
  345.8 79.8 %copy-start.2 = (bf16[128,2048]{1,0:T(8,128)(2,1)S(1)}, bf16[128,2048]{1,0:T(8,128)(2,1)}, u32[]{:S(2)}) copy-start(bf16[128,2048]{1,0:T(8,128)(2,1)} %param.9) | copy-start | bytes 1572868
  421.9 154.9 %all-to-all-start.2 = ((bf16[32,36,2048]{2,1,0:T(8,128)(2,1)}), bf16[32,36,2048]{2,1,0:T(8,128)(2,1)}, u32[]{:S(2)}, u32[]{:S(2)}) async-start(bf16[32,36,2048]{2,1,0:T(8,128)(2,1)} %reshape.151), calls=%async_computation.2 | async-start | bytes 10485760 | tf_op jit(solution)/shard_map/all_to_all | solution.py:166
  425.5 78.3 %all-reduce.3.cloned.1.call-start = ((), (), s32[]{:S(2)}) async-start(), calls=%async_computation.5 | async-start | bytes 524288 | tf_op jit(solution)/shard_map/psum | solution.py:181
  426.6 124.7 %all-reduce.5.cloned.1.call-start = ((), (), s32[]{:S(2)}) async-start(), calls=%async_computation.6 | async-start | bytes 524288 | tf_op jit(solution)/shard_map/psum | solution.py:181
  553.0 9.1 %copy-start.9 = (bf16[1,1152,768]{2,1,0:T(8,128)(2,1)S(1)}, bf16[1,1152,768]{2,1,0:T(8,128)(2,1)}, u32[]{:S(2)}) copy-start(bf16[1,1152,768]{2,1,0:T(8,128)(2,1)} %param.14) | copy-start | bytes 5308420
  553.0 9.1 %copy-start.11 = (bf16[1,1152,768]{2,1,0:T(8,128)(2,1)S(1)}, bf16[1,1152,768]{2,1,0:T(8,128)(2,1)}, u32[]{:S(2)}) copy-start(bf16[1,1152,768]{2,1,0:T(8,128)(2,1)} %param.13) | copy-start | bytes 5308420
  562.0 8.5 %copy-start.3 = (bf16[1152,2048]{1,0:T(8,128)(2,1)S(1)}, bf16[1152,2048]{1,0:T(8,128)(2,1)}, u32[]{:S(2)}) copy-start(bf16[1152,2048]{1,0:T(8,128)(2,1)} %reshape.156) | copy-start | bytes 14155780
  562.0 8.5 %copy-start.12 = (f32[1152,768]{1,0:T(8,128)S(1)}, f32[1152,768]{1,0:T(8,128)}, u32[]{:S(2)}) copy-start(f32[1152,768]{1,0:T(8,128)} %get-tuple-element.10) | copy-start | bytes 10616836
  576.8 11.8 %copy-start.1 = (bf16[1,768,2048]{2,1,0:T(8,128)(2,1)S(1)}, bf16[1,768,2048]{2,1,0:T(8,128)(2,1)}, u32[]{:S(2)}) copy-start(bf16[1,768,2048]{2,1,0:T(8,128)(2,1)} %param.17) | copy-start | bytes 9437188
  584.2 3.3 copy-start.5
Sparse Core Ops, SparseCore 0:
  429.3 74.5 all-reduce.2
  507.0 44.2 all-reduce.4
